TPU v7x, 32 devices: a whole 2x2x4 slice. The times are simulated.
32 devices in a mesh: seq: 8 (over z, x), win: 4 (over y, core).
Axes of the slice: x: 2, y: 2, z: 4, core: 2. Of those that a mesh axis runs over, the one named last changes fastest.
Arguments:
- inputs: bfloat16 [4, 3072, 1536], P('win', 'seq'), may hold values from -6 to 6
- cotangent: bfloat16 [4, 3072, 1536], P('win', 'seq'), may hold values from -6 to 6
- w_dilated: bfloat16 [2, 1536, 3, 768], P(None, ('seq', 'win')), may hold values from -0.09375 to 0.09375
- w_mix: bfloat16 [2, 1536, 768], P(None, ('seq', 'win')), may hold values from -0.21875 to 0.21875
- in_scale: float32 [2, 1536], replicated, may hold values from 0.1 to 1.9
- in_shift: float32 [2, 1536], replicated, may hold values from -3 to 3
- mid_scale: float32 [2, 768], replicated, may hold values from 0.1 to 1.9
- mid_shift: float32 [2, 768], replicated, may hold values from -3 to 3
Outputs:
- output: bfloat16 [4, 3072, 1536], P('win', 'seq')
- input_gradient: float32 [4, 3072, 1536], P('win', 'seq')
- dilated_weight_gradient: float32 [2, 1536, 3, 768], P(None, ('seq', 'win'))
- grad_mix: float32 [2, 1536, 768], P(None, ('seq', 'win'))
All inputs are finite; a program needn't handle non-finite values.
Results may differ from a plain program's by a relative error of at most 0.034.
Values may be sent and summed in bfloat16 or wider, within the bound.
No kernel may reach another device: no remote copies, remote signals or barrier semaphores. Data moves between devices by JAX's collectives and lax.ppermute only.
A program may use at most 192 MiB of HBM per device.

v0:
```python
import math
import jax
import jax.numpy as jnp
from jax import lax
from jax.sharding import PartitionSpec as P

dilation_steps = (8, 16)


def padded_2(block, sides, width):
    for axis, dim in sides:
        count = lax.axis_size(axis)
        forward = [(i, i + 1) for i in range(count - 1)]
        backward = [(target, source) for source, target in forward]
        low = lax.ppermute(
            lax.slice_in_dim(block, block.shape[dim] - width, None, axis=dim), axis, forward
        )
        high = lax.ppermute(lax.slice_in_dim(block, 0, width, axis=dim), axis, backward)
        block = jnp.concatenate([low, block, high], axis=dim)
    return block


def gelu_value(values):
    return jax.nn.gelu(values, approximate=True)


def gelu_back(pre_values, upstream_gradient):
    return jax.vjp(gelu_value, pre_values)[1](upstream_gradient)[0]


def dilated_conv(padded, w_conv, dilation, out_rows):
    hidden = jnp.dot(padded[0:out_rows], w_conv[:, 0, :], preferred_element_type=jnp.float32)
    for kernel_tap in (1, 2):
        lower = kernel_tap * dilation
        hidden = hidden + jnp.dot(
            padded[lower : lower + out_rows],
            w_conv[:, kernel_tap, :],
            preferred_element_type=jnp.float32,
        )
    return hidden


def fetch_weights(w_dilated, w_mix):
    blocks, rows, taps, c2 = w_dilated.shape
    local = jnp.concatenate(
        [
            w_dilated.reshape(blocks, rows, taps * c2).transpose(1, 0, 2).reshape(rows, -1),
            w_mix.transpose(1, 0, 2).reshape(rows, -1),
        ],
        axis=1,
    )
    gathered = lax.all_gather(local, ("seq", "win"), axis=0, tiled=True)
    full_rows = gathered.shape[0]
    split = blocks * taps * c2
    return [
        (
            gathered[:, b * taps * c2 : (b + 1) * taps * c2].reshape(full_rows, taps, c2),
            gathered[:, split + b * c2 : split + (b + 1) * c2],
        )
        for b in range(blocks)
    ]


def weight_gradient_terms(padded, d_hidden, cot_here, middle, dilation, inverse_square_root):
    row_count = d_hidden.shape[0]
    kernel_taps = [
        jnp.einsum(
            "pc,pe->ce",
            padded[kernel_tap * dilation : kernel_tap * dilation + row_count],
            d_hidden,
            preferred_element_type=jnp.float32,
        )
        for kernel_tap in range(3)
    ]
    dilated = (jnp.concatenate(kernel_taps, axis=1) * inverse_square_root).astype(jnp.bfloat16)
    mixed = (
        jnp.einsum("pc,pe->ce", cot_here, middle, preferred_element_type=jnp.float32)
        * inverse_square_root
    ).astype(jnp.bfloat16)
    return (dilated, mixed)


def per_device(inputs, cotangent, w_dilated, w_mix, in_scale, in_shift, mid_scale, mid_shift):
    x_local = inputs[0]
    cot_local = cotangent[0]
    row_count = x_local.shape[0]
    window_len = lax.axis_size("seq") * row_count
    inverse_square_root = 1.0 / math.sqrt(lax.axis_size("win") * inputs.shape[0] * window_len)
    residual_block_count = len(dilation_steps)
    saved = []
    weights = fetch_weights(w_dilated, w_mix)
    stream = x_local.astype(jnp.float32)
    for residual_block_index in range(residual_block_count):
        dilation = dilation_steps[residual_block_index]
        w_conv, w_out = weights[residual_block_index]
        pre_in = stream * in_scale[residual_block_index] + in_shift[residual_block_index]
        activated = gelu_value(pre_in).astype(jnp.bfloat16)
        padded = padded_2(activated, (("seq", 0),), dilation)
        pre_mid = (
            dilated_conv(padded, w_conv, dilation, row_count) * mid_scale[residual_block_index]
            + mid_shift[residual_block_index]
        )
        middle = gelu_value(pre_mid).astype(jnp.bfloat16)
        stream = stream + jnp.einsum("pe,ce->pc", middle, w_out, preferred_element_type=jnp.float32)
        saved.append((w_conv, w_out, pre_in, padded, pre_mid, middle))
    output = stream.astype(jnp.bfloat16)
    upstream_gradient = cot_local.astype(jnp.float32)
    dilated_weight_gradients = [None] * residual_block_count
    mixing_weight_gradients = [None] * residual_block_count
    for residual_block_index in reversed(range(residual_block_count)):
        dilation = dilation_steps[residual_block_index]
        w_conv, w_out, pre_in, padded, pre_mid, middle = saved[residual_block_index]
        cot_here = upstream_gradient.astype(jnp.bfloat16)
        d_mid = jnp.dot(cot_here, w_out, preferred_element_type=jnp.float32)
        d_hidden = (gelu_back(pre_mid, d_mid) * mid_scale[residual_block_index]).astype(
            jnp.bfloat16
        )
        d_pad = padded_2(d_hidden, (("seq", 0),), dilation)
        d_act = jnp.einsum(
            "pe,ce->pc",
            d_pad[2 * dilation : 2 * dilation + row_count],
            w_conv[:, 0, :],
            preferred_element_type=jnp.float32,
        )
        for kernel_tap in (1, 2):
            lower = (2 - kernel_tap) * dilation
            d_act = d_act + jnp.einsum(
                "pe,ce->pc",
                d_pad[lower : lower + row_count],
                w_conv[:, kernel_tap, :],
                preferred_element_type=jnp.float32,
            )
        (
            dilated_weight_gradients[residual_block_index],
            mixing_weight_gradients[residual_block_index],
        ) = weight_gradient_terms(padded, d_hidden, cot_here, middle, dilation, inverse_square_root)
        upstream_gradient = (
            upstream_gradient + gelu_back(pre_in, d_act) * in_scale[residual_block_index]
        )
    summed = lax.psum_scatter(
        jnp.concatenate(dilated_weight_gradients + mixing_weight_gradients, axis=1),
        ("seq", "win"),
        scatter_dimension=0,
        tiled=True,
    ).astype(jnp.float32)
    own_rows = summed.shape[0]
    taps, c2 = (w_dilated.shape[2], w_dilated.shape[3])
    split = residual_block_count * taps * c2
    return (
        output[None],
        upstream_gradient[None],
        summed[:, :split].reshape(own_rows, residual_block_count, taps, c2).transpose(1, 0, 2, 3),
        summed[:, split:].reshape(own_rows, residual_block_count, c2).transpose(1, 0, 2),
    )


def solution(mesh):
    in_specs = (
        P("win", "seq", None),
        P("win", "seq", None),
        P(None, ("seq", "win"), None, None),
        P(None, ("seq", "win"), None),
        P(),
        P(),
        P(),
        P(),
    )
    out_specs = (
        P("win", "seq", None),
        P("win", "seq", None),
        P(None, ("seq", "win"), None, None),
        P(None, ("seq", "win"), None),
    )
    return jax.shard_map(
        per_device, mesh=mesh, in_specs=in_specs, out_specs=out_specs, check_vma=False
    )
```

profile of v0, /device:TPU:0, one launch (start us, length us, event | category | flops | bytes accessed | tf_op | source)
XLA Modules:
  0.0 499.8 jit_solution(18363902650150961037)
XLA Ops:
  7.2 0.0 all-gather.2.cloned.1.call-start
  7.2 1.0 copy.44
  8.3 1.0 copy.42
  9.3 0.0 copy-start.4
  9.4 0.0 copy-start.5
  9.4 0.9 pad_maximum_fusion.21
  10.2 0.0 all-gather.2.cloned.1.call-update
  10.2 0.0 reduce-scatter.4.cloned.1.call-start
  10.3 0.1 slice_reduce_fusion
  10.4 1.0 fusion.14
  11.4 1.3 collective-permute-start.1
  12.7 5.5 %collective-permute-start = (bf16[8,1536]{1,0:T(8,128)(2,1)S(1)}, bf16[8,1536]{1,0:T(8,128)(2,1)S(1)}, u32[]{:S(2)}, u32[]{:S(2)}) collective-permute-start(bf16[8,1536]{1,0:T(8,128)(2,1)S(1)} %get-tuple-element.16), channel_id=1, source_target_pairs={{0,4},{4,8},{8,12},{12,16},{16,20},{20,24},{24,28},{1,5},{5,9},{9,... | collective-permute-start | bytes 73736 | tf_op jit(solution)/shard_map/ppermute | solution.py:15
  18.2 120.7 %all-gather.2.cloned.1.call-done = bf16[1536,6144]{1,0:T(8,128)(2,1)} async-done(((bf16[48,6144]{1,0:T(8,128)(2,1)}), bf16[1536,6144]{1,0:T(8,128)(2,1)}) %all-gather.2.cloned.1.call-update) | async-done | bytes 18874384 | tf_op jit(solution)/shard_map/all_gather | solution.py:52
  138.9 10.1 %fusion.125 = (bf16[1536,2304]{1,0:T(8,128)(2,1)}, bf16[1536,2304]{1,0:T(8,128)(2,1)}) fusion(bf16[1536,6144]{1,0:T(8,128)(2,1)} %all-gather.2.cloned.1.call-done), kind=kLoop, calls=%fused_computation.163 | loop fusion | bytes 28311552 | tf_op jit(solution)/shard_map/slice | solution.py:57
  149.0 10.2 %copy.30 = bf16[1536,2304]{0,1:T(8,128)(2,1)} copy(bf16[1536,2304]{1,0:T(8,128)(2,1)} %get-tuple-element.13) | data formatting | bytes 14155776 | tf_op jit(solution)/shard_map/slice | solution.py:57
  159.2 4.4 fusion.42
  163.6 3.8 fusion.44
  167.4 10.3 %copy.34 = bf16[1536,2304]{0,1:T(8,128)(2,1)} copy(bf16[1536,2304]{1,0:T(8,128)(2,1)} %get-tuple-element.12) | data formatting | bytes 14155776 | tf_op jit(solution)/shard_map/slice | solution.py:57
  177.7 0.0 collective-permute-done
  177.7 3.6 fusion.66
  181.3 3.6 multiply_convert_fusion.2
  185.0 0.0 copy-start.9
  185.0 1.3 collective-permute-start.3
  186.3 1.1 fusion.47
  187.4 4.7 collective-permute-start.2
  192.2 1.1 fusion.49
  193.3 0.4 collective-permute-done.2
  193.7 1.1 fusion.62
  194.8 0.1 copy-done.6
  195.0 3.0 fusion.2
  197.9 3.3 fusion.82
  201.2 1.5 fusion.131
  202.7 4.2 collective-permute-start.5
  206.9 1.5 fusion.102
  208.4 1.5 fusion.101
  209.9 4.3 fusion.1
  214.2 1.1 fusion.46
  215.3 1.5 collective-permute-start.4
  216.8 1.1 fusion.48
  217.9 4.3 collective-permute-done.4
  222.2 2.7 fusion.38
  224.9 2.9 multiply_convert_fusion.1
  227.9 3.3 fusion.74
  231.1 1.5 fusion.130
  232.6 1.4 fusion.100
  234.0 1.5 fusion.99
  235.5 4.3 fusion
  239.7 17.0 %pad_maximum_fusion = bf16[1536,6144]{0,1:T(8,128)(2,1)} fusion(bf16[1536,768]{0,1:T(8,128)(2,1)} %fusion.2, bf16[1536,768]{0,1:T(8,128)(2,1)} %multiply_convert_fusion.1, bf16[1536,2304]{0,1:T(8,128)(2,1)} %fusion.1, bf16[1536,2304]{0,1:T(8,128)(2,1)} %fusion), kind=kLoop, calls=%fused_computation | loop fusion | flops 75497472 | bytes 37748736 | tf_op jit(solution)/shard_map/concatenate | solution.py:141
  256.7 24.7 %copy.40 = bf16[1536,6144]{1,0:T(8,128)(2,1)} copy(bf16[1536,6144]{0,1:T(8,128)(2,1)} %pad_maximum_fusion) | data formatting | bytes 37748736
  281.5 0.0 reduce-scatter.4.cloned.1.call-update
  281.5 1.2 copy-done.11
  282.7 4.6 fusion.7
  287.3 5.1 %collective-permute-start.7 = (bf16[8,768]{1,0:T(8,128)(2,1)S(1)}, bf16[8,768]{1,0:T(8,128)(2,1)S(1)}, u32[]{:S(2)}, u32[]{:S(2)}) collective-permute-start(bf16[8,768]{1,0:T(8,128)(2,1)S(1)} %get-tuple-element.19), channel_id=1, source_target_pairs={{0,4},{4,8},{8,12},{12,16},{16,20},{20,24},{24,28},{1,5},{5,9},{9,... | collective-permute-start | bytes 36872 | tf_op jit(solution)/shard_map/ppermute | solution.py:15
  292.4 2.9 fusion.41
  295.3 1.6 collective-permute-start.6
  296.9 2.9 fusion.43
  299.8 1.4 collective-permute-done.6
  301.2 5.9 %fusion.30 = f32[1,384,1536]{2,1,0:T(8,128)} fusion(f32[384,1536]{1,0:T(8,128)S(1)} %copy-done.8, bf16[1,384,1536]{2,1,0:T(8,128)(2,1)S(1)} %copy-done.1, f32[384,1536]{1,0:T(8,128)S(1)} %fusion.43, f32[384,1536]{1,0:T(8,128)S(1)} %fusion.41, bf16[1536,3,768]{0,2,1:T(8,128)(2,1)} %bitcast.154, f32[1536]{0:T(1024)S(1)} %get-tuple-element.7, ...), kind=kOutput, calls=%fused_computation.46 | convolution fusion | flops 922484736 | bytes 13590528 | tf_op jit(solution)/shard_map/pe,ce->pc/dot_general | solution.py:119
  307.1 180.9 %reduce-scatter.4.cloned.1.call-done = bf16[48,6144]{1,0:T(8,128)(2,1)} async-done(((bf16[1536,6144]{1,0:T(8,128)(2,1)}), bf16[48,6144]{1,0:T(8,128)(2,1)}) %reduce-scatter.4.cloned.1.call-update) | async-done | bytes 589840
  488.1 1.1 slice.184
  489.1 0.8 copy.45
  490.0 1.6 copy.38
  491.7 0.3 copy.46
  492.0 1.0 copy.39
  (35 shorter events, 0.2 us)
Async XLA Ops:
  7.2 3.1 copy-start.2
  7.2 3.1 copy-start.3
  7.2 3.2 copy-start.1
  7.2 131.7 %all-gather.2.cloned.1.call-start = ((), (), s32[]{:S(2)}) async-start(), calls=%async_computation.1 | async-start | bytes 19464192 | tf_op jit(solution)/shard_map/all_gather | solution.py:52
  9.3 8.8 %copy-start.4 = (f32[2,768]{1,0:T(2,128)S(1)}, f32[2,768]{1,0:T(2,128)}, u32[]{:S(2)}) copy-start(f32[2,768]{1,0:T(2,128)} %param.15) | copy-start | bytes 18436
  9.4 8.8 %copy-start.5 = (f32[2,768]{1,0:T(2,128)S(1)}, f32[2,768]{1,0:T(2,128)}, u32[]{:S(2)}) copy-start(f32[2,768]{1,0:T(2,128)} %param.14) | copy-start | bytes 18436
  10.2 477.8 %reduce-scatter.4.cloned.1.call-start = ((), (), s32[]{:S(2)}) async-start(), calls=%async_computation.2 | async-start | bytes 19464192
  11.4 152.2 %collective-permute-start.1 = (bf16[8,1536]{1,0:T(8,128)(2,1)S(1)}, bf16[8,1536]{1,0:T(8,128)(2,1)S(1)}, u32[]{:S(2)}, u32[]{:S(2)}) collective-permute-start(bf16[8,1536]{1,0:T(8,128)(2,1)S(1)} %get-tuple-element.17), channel_id=1, source_target_pairs={{4,0},{8,4},{12,8},{16,12},{20,16},{24,20},{28,24},{5,1},{9,5},{13... | collective-permute-start | bytes 73736 | tf_op jit(solution)/shard_map/ppermute | solution.py:18
  12.7 165.0 %collective-permute-start = (bf16[8,1536]{1,0:T(8,128)(2,1)S(1)}, bf16[8,1536]{1,0:T(8,128)(2,1)S(1)}, u32[]{:S(2)}, u32[]{:S(2)}) collective-permute-start(bf16[8,1536]{1,0:T(8,128)(2,1)S(1)} %get-tuple-element.16), channel_id=1, source_target_pairs={{0,4},{4,8},{8,12},{12,16},{16,20},{20,24},{24,28},{1,5},{5,9},{9,... | collective-permute-start | bytes 73736 | tf_op jit(solution)/shard_map/ppermute | solution.py:15
  177.7 8.6 %slice-start = ((s8[7077888]{0:T(1024)(128)(4,1)}), s8[4194304]{0:T(1024)(128)(4,1)S(1)}, s32[]{:S(2)}) async-start(s8[7077888]{0:T(1024)(128)(4,1)} %bitcast.155), calls=%async_computation.3 | async-start | bytes 8388608
  181.3 5.0 slice-start.1
  185.0 37.3 %copy-start.9 = (f32[384,1536]{1,0:T(8,128)}, f32[384,1536]{1,0:T(8,128)S(1)}, u32[]{:S(2)}) copy-start(f32[384,1536]{1,0:T(8,128)S(1)} %get-tuple-element.23) | copy-start | bytes 7077892
  185.0 7.2 %collective-permute-start.3 = (bf16[16,1536]{1,0:T(8,128)(2,1)S(1)}, bf16[16,1536]{1,0:T(8,128)(2,1)S(1)}, u32[]{:S(2)}, u32[]{:S(2)}) collective-permute-start(bf16[16,1536]{1,0:T(8,128)(2,1)S(1)} %get-tuple-element.15), channel_id=1, source_target_pairs={{4,0},{8,4},{12,8},{16,12},{20,16},{24,20},{28,24},{5,1},{9,5},{13... | collective-permute-start | bytes 147464 | tf_op jit(solution)/shard_map/ppermute | solution.py:18
  187.4 6.3 %collective-permute-start.2 = (bf16[16,1536]{1,0:T(8,128)(2,1)S(1)}, bf16[16,1536]{1,0:T(8,128)(2,1)S(1)}, u32[]{:S(2)}, u32[]{:S(2)}) collective-permute-start(bf16[16,1536]{1,0:T(8,128)(2,1)S(1)} %get-tuple-element.14), channel_id=1, source_target_pairs={{0,4},{4,8},{8,12},{12,16},{16,20},{20,24},{24,28},{1,5},{5,9},{9,... | collective-permute-start | bytes 147464 | tf_op jit(solution)/shard_map/ppermute | solution.py:15
  193.7 1.3 copy-start.6
  195.0 3.0 copy-start.10
  202.7 14.1 %collective-permute-start.5 = (bf16[16,768]{1,0:T(8,128)(2,1)S(1)}, bf16[16,768]{1,0:T(8,128)(2,1)S(1)}, u32[]{:S(2)}, u32[]{:S(2)}) collective-permute-start(bf16[16,768]{1,0:T(8,128)(2,1)S(1)} %get-tuple-element.21), channel_id=1, source_target_pairs={{0,4},{4,8},{8,12},{12,16},{16,20},{20,24},{24,28},{1,5},{5,9},{9,... | collective-permute-start | bytes 73736 | tf_op jit(solution)/shard_map/ppermute | solution.py:15
  215.3 6.9 %collective-permute-start.4 = (bf16[16,768]{1,0:T(8,128)(2,1)S(1)}, bf16[16,768]{1,0:T(8,128)(2,1)S(1)}, u32[]{:S(2)}, u32[]{:S(2)}) collective-permute-start(bf16[16,768]{1,0:T(8,128)(2,1)S(1)} %get-tuple-element.20), channel_id=1, source_target_pairs={{4,0},{8,4},{12,8},{16,12},{20,16},{24,20},{28,24},{5,1},{9,5},{13... | collective-permute-start | bytes 73736 | tf_op jit(solution)/shard_map/ppermute | solution.py:18
  224.9 2.9 copy-start.7
  281.5 1.3 copy-start.11
  287.3 9.6 %collective-permute-start.7 = (bf16[8,768]{1,0:T(8,128)(2,1)S(1)}, bf16[8,768]{1,0:T(8,128)(2,1)S(1)}, u32[]{:S(2)}, u32[]{:S(2)}) collective-permute-start(bf16[8,768]{1,0:T(8,128)(2,1)S(1)} %get-tuple-element.19), channel_id=1, source_target_pairs={{0,4},{4,8},{8,12},{12,16},{16,20},{20,24},{24,28},{1,5},{5,9},{9,... | collective-permute-start | bytes 36872 | tf_op jit(solution)/shard_map/ppermute | solution.py:15
  295.3 5.9 %copy-start.8 = (f32[384,1536]{1,0:T(8,128)S(1)}, f32[384,1536]{1,0:T(8,128)}, u32[]{:S(2)}) copy-start(f32[384,1536]{1,0:T(8,128)} %copy-done.7) | copy-start | bytes 7077892
  295.3 5.9 %collective-permute-start.6 = (bf16[8,768]{1,0:T(8,128)(2,1)S(1)}, bf16[8,768]{1,0:T(8,128)(2,1)S(1)}, u32[]{:S(2)}, u32[]{:S(2)}) collective-permute-start(bf16[8,768]{1,0:T(8,128)(2,1)S(1)} %get-tuple-element.18), channel_id=1, source_target_pairs={{4,0},{8,4},{12,8},{16,12},{20,16},{24,20},{28,24},{5,1},{9,5},{13... | collective-permute-start | bytes 36872 | tf_op jit(solution)/shard_map/ppermute | solution.py:18
  490.0 1.7 copy-start
Sparse Core Ops, SparseCore 0:
  11.5 127.3 all-gather.1
  281.6 206.4 reduce-scatter.3
where the time goes:
time: 502 us; the launch traced here: 500 us
  waiting for transfers between devices  308 us (61%)
  local copies, waits for them, and re-layouts  63.7 us (13%)
  matrix products  61.1 us (12%)
  other arithmetic  27.4 us (5%)
  starting transfers between devices  25.2 us (5%)
  between operations  14.5 us (3%)
    unnamed x3, waiting for transfers between devices  181 us
    all_gather x1, waiting for transfers between devices, fetch_weights(): gathered = lax.all_gather(local, ('seq', 'win'), axis=0, tiled=True)  121 us
    slice x3, local copies, waits for them, and re-layouts, fetch_weights(): gathered[:, b * taps * c2:(b + 1) * taps * c2].reshape(full_rows, taps, c2)  30.6 us
    unnamed x31, local copies, waits for them, and re-layouts  27.3 us
    ppermute x4, starting transfers between devices, padded_2(): lax.ppermute(lax.slice_in_dim(block, block.shape[dim] - width, None, axis...  19.5 us
    concatenate x1, other arithmetic, per_device(): jnp.concatenate(dilated_weight_gradients + mixing_weight_gradients, axis=1)  17 us
    dot_general x4, matrix products, dilated_conv(): jnp.dot(padded[lower:lower + out_rows], w_conv[:, kernel_tap, :], preferr...  10.4 us
  transfers between devices with their start and end apart: 10, of which 5 were waited for; matrix products, arithmetic and copies ran while one was open for 14% of the time, Pallas kernels for 0%

commit v1 on v0

--- a/solution.py
+++ b/solution.py
@@ -5,6 +5,30 @@
 from jax.sharding import PartitionSpec as P
 
 dilation_steps = (8, 16)
+
+
+def cover_links(row_data, d_out):
+    row_data = jnp.moveaxis(row_data, 0, d_out)
+    known = row_data.shape
+    return row_data.reshape(*known[:d_out], known[d_out] * known[d_out + 1], *known[d_out + 2 :])
+
+
+def fill_sections(incoming_x, which_axis):
+    amount_of = lax.psum(1, which_axis)
+    u_next = incoming_x[None]
+    for j in range(amount_of.bit_length() - 1):
+        arr_next = 1 << j
+        next_value = lax.ppermute(
+            u_next, which_axis, perm=tuple(((s, s ^ arr_next) for s in range(amount_of)))
+        )
+        local_now = jnp.stack([u_next, next_value], axis=0)
+        v1 = lax.axis_index(which_axis) >> j & 1
+        u_next = jnp.where(v1 == 0, local_now, local_now[::-1]).reshape(-1, *incoming_x.shape)
+    return u_next
+
+
+def write_rounds(local_block, matrix, array_dim):
+    return cover_links(fill_sections(local_block, matrix), array_dim)
 
 
 def padded_2(block, sides, width):
@@ -49,7 +73,7 @@
         ],
         axis=1,
     )
-    gathered = lax.all_gather(local, ("seq", "win"), axis=0, tiled=True)
+    gathered = write_rounds(local, ("seq", "win"), 0)
     full_rows = gathered.shape[0]
     split = blocks * taps * c2
     return [

time: 502 us -> 1020 us (2.03); the launches traced: 500 us -> 1010 us
  waiting for transfers between devices: 308 us -> 763 us
  other arithmetic: 27.4 us -> 70.8 us
    ppermute x0 -> x5, waiting for transfers between devices: none -> 576 us  [fill_sections(): lax.ppermute(u_next, which_axis, perm=tuple(((s, s ^ arr_next) for s in r...]
    all_gather x1 -> x0, waiting for transfers between devices: 121 us -> none  [fetch_weights(): gathered = lax.all_gather(local, ('seq', 'win'), axis=0, tiled=True)]
    select_n x0 -> x4, other arithmetic: none -> 24.1 us  [fill_sections(): jnp.where(v1 == 0, local_now, local_now[::-1])]
    another operation x0 -> x6, other arithmetic: none -> 20.2 us  [fill_sections(): local_now = jnp.stack([u_next, next_value], axis=0)]
    unnamed x31 -> x42, local copies, waits for them, and re-layouts: 27.3 us -> 31.2 us
    unnamed x3 -> x2, waiting for transfers between devices: 181 us -> 181 us
  transfers between devices with their start and end apart: 10 -> 14, of which waited for: 5 -> 9; matrix products, arithmetic and copies ran while one was open for 14% -> 8% of each run, Pallas kernels for 0% -> 0%
where the time goes in v1:
time: 1020 us; the launch traced here: 1010 us
  waiting for transfers between devices  763 us (75%)
  other arithmetic  70.8 us (7%)
  local copies, waits for them, and re-layouts  63 us (6%)
  matrix products  62.5 us (6%)
  starting transfers between devices  33.7 us (3%)
  between operations  14.8 us (1%)
    ppermute x5, waiting for transfers between devices, fill_sections(): lax.ppermute(u_next, which_axis, perm=tuple(((s, s ^ arr_next) for s in r...  576 us
    unnamed x2, waiting for transfers between devices  181 us
    unnamed x42, local copies, waits for them, and re-layouts  31.2 us
    slice x3, local copies, waits for them, and re-layouts, fetch_weights(): gathered[:, b * taps * c2:(b + 1) * taps * c2].reshape(full_rows, taps, c2)  26.9 us
    select_n x4, other arithmetic, fill_sections(): jnp.where(v1 == 0, local_now, local_now[::-1])  24.1 us
  transfers between devices with their start and end apart: 14, of which 9 were waited for; matrix products, arithmetic and copies ran while one was open for 8% of the time, Pallas kernels for 0%

profile of v1, /device:TPU:0, one launch (start us, length us, event | category | flops | bytes accessed | tf_op | source)
XLA Modules:
  0.0 1007.4 jit_solution(9190054750917532734)
XLA Ops:
  7.2 1.1 copy.56
  8.9 1.6 collective-permute-done.1
  11.0 3.0 collective-permute-start.2
  13.9 26.3 %collective-permute-done.2 = bf16[2,48,6144]{2,1,0:T(8,128)(2,1)S(1)} collective-permute-done((bf16[2,48,6144]{2,1,0:T(8,128)(2,1)S(1)}, bf16[2,48,6144]{2,1,0:T(8,128)(2,1)S(1)}, u32[]{:S(2)}, u32[]{:S(2)}) %collective-permute-start.2) | collective-permute-done | bytes 1179680 | tf_op jit(solution)/shard_map/ppermute | solution.py:21
  40.9 1.8 collective-permute-start.3
  42.7 51.2 %collective-permute-done.3 = bf16[4,48,6144]{2,1,0:T(8,128)(2,1)} collective-permute-done((bf16[4,48,6144]{2,1,0:T(8,128)(2,1)S(1)}, bf16[4,48,6144]{2,1,0:T(8,128)(2,1)}, u32[]{:S(2)}, u32[]{:S(2)}) %collective-permute-start.3) | collective-permute-done | bytes 2359328 | tf_op jit(solution)/shard_map/ppermute | solution.py:21
  93.8 2.1 pad_maximum_fusion.3
  95.9 3.4 reverse_select_fusion.2
  99.3 1.5 collective-permute-start.4
  100.8 101.3 %collective-permute-done.4 = bf16[8,48,6144]{2,1,0:T(8,128)(2,1)} collective-permute-done((bf16[8,48,6144]{2,1,0:T(8,128)(2,1)}, bf16[8,48,6144]{2,1,0:T(8,128)(2,1)}, u32[]{:S(2)}, u32[]{:S(2)}) %collective-permute-start.4) | collective-permute-done | bytes 4718624 | tf_op jit(solution)/shard_map/ppermute | solution.py:21
  202.1 8.3 pad_maximum_fusion.2
  210.4 14.9 %reverse_select_fusion.1 = bf16[2,8,48,6144]{3,2,1,0:T(8,128)(2,1)} fusion(bf16[2,8,48,6144]{3,2,1,0:T(8,128)(2,1)} %pad_maximum_fusion.2, pred[]{:T(512)S(6)} %eq.16), kind=kLoop, calls=%fused_computation.7 | loop fusion | flops 4718592 | bytes 18874368 | tf_op jit(solution)/shard_map/jit(_where)/select_n | solution.py:26
  225.3 2.2 collective-permute-start.5
  228.5 1.0 copy-done.1
  229.5 1.3 collective-permute-start.6
  230.8 5.1 collective-permute-start
  235.9 395.7 %collective-permute-done.5 = bf16[16,48,6144]{2,1,0:T(8,128)(2,1)} collective-permute-done((bf16[16,48,6144]{2,1,0:T(8,128)(2,1)}, bf16[16,48,6144]{2,1,0:T(8,128)(2,1)}, u32[]{:S(2)}, u32[]{:S(2)}) %collective-permute-start.5) | collective-permute-done | bytes 9437216 | tf_op jit(solution)/shard_map/ppermute | solution.py:21
  631.6 9.2 pad_maximum_fusion
  640.9 5.3 reverse_select_fusion
  646.2 6.3 fusion.127
  652.5 4.4 copy-done
  656.9 10.4 %copy.44 = bf16[1536,2304]{0,1:T(8,128)(2,1)} copy(bf16[1536,2304]{1,0:T(8,128)(2,1)} %get-tuple-element.13) | data formatting | bytes 14155776 | tf_op jit(solution)/shard_map/slice | solution.py:81
  667.3 4.5 fusion.42
  671.8 3.8 fusion.44
  675.6 10.3 %copy.48 = bf16[1536,2304]{0,1:T(8,128)(2,1)} copy(bf16[1536,2304]{1,0:T(8,128)(2,1)} %get-tuple-element.12) | data formatting | bytes 14155776 | tf_op jit(solution)/shard_map/slice | solution.py:81
  685.9 3.6 fusion.66
  689.5 3.6 multiply_convert_fusion.2
  693.2 1.3 collective-permute-start.8
  694.6 1.1 fusion.47
  695.7 4.7 collective-permute-start.7
  700.4 1.1 fusion.49
  702.0 1.1 fusion.62
  703.2 3.7 fusion.82
  706.9 3.0 fusion.2
  709.9 1.5 fusion.133
  711.4 4.2 collective-permute-start.10
  715.6 1.5 fusion.104
  717.1 1.5 fusion.103
  718.5 4.2 fusion.1
  722.8 1.1 fusion.46
  723.8 1.5 collective-permute-start.9
  725.4 1.1 fusion.48
  726.4 3.4 collective-permute-done.9
  729.8 2.7 fusion.38
  732.5 4.1 fusion.74
  736.6 2.9 multiply_convert_fusion.1
  739.6 1.4 fusion.132
  741.0 1.4 fusion.102
  742.5 1.5 fusion.101
  743.9 4.3 fusion
  748.3 16.9 %pad_maximum_fusion.1 = bf16[1536,6144]{0,1:T(8,128)(2,1)} fusion(bf16[1536,768]{0,1:T(8,128)(2,1)} %fusion.2, bf16[1536,768]{0,1:T(8,128)(2,1)} %multiply_convert_fusion.1, bf16[1536,2304]{0,1:T(8,128)(2,1)} %fusion.1, bf16[1536,2304]{0,1:T(8,128)(2,1)} %fusion), kind=kLoop, calls=%fused_computation.2 | loop fusion | flops 75497472 | bytes 37748736 | tf_op jit(solution)/shard_map/concatenate | solution.py:165
  765.2 23.1 %copy.54 = bf16[1536,6144]{1,0:T(8,128)(2,1)} copy(bf16[1536,6144]{0,1:T(8,128)(2,1)} %pad_maximum_fusion.1) | data formatting | bytes 37748736
  788.3 1.2 copy-done.16
  789.6 4.6 fusion.7
  794.2 5.1 collective-permute-start.12
  799.2 3.0 fusion.41
  802.2 1.6 collective-permute-start.11
  803.8 2.9 fusion.43
  806.7 1.3 collective-permute-done.11
  808.1 6.0 fusion.30
  814.0 181.4 %reduce-scatter.4.cloned.1.call-done = bf16[48,6144]{1,0:T(8,128)(2,1)} async-done(((bf16[1536,6144]{1,0:T(8,128)(2,1)}), bf16[48,6144]{1,0:T(8,128)(2,1)}) %reduce-scatter.4.cloned.1.call-update) | async-done | bytes 589840
  995.4 1.1 slice.184
  997.3 1.6 copy.52
  999.3 1.0 copy.53
  (63 shorter events, 4.6 us)
Async XLA Ops:
  7.2 1.2 copy-start.6
  7.2 988.2 %reduce-scatter.4.cloned.1.call-start = ((), (), s32[]{:S(2)}) async-start(), calls=%async_computation.1 | async-start | bytes 19464192
  8.4 2.1 collective-permute-start.1
  11.0 29.2 %collective-permute-start.2 = (bf16[2,48,6144]{2,1,0:T(8,128)(2,1)S(1)}, bf16[2,48,6144]{2,1,0:T(8,128)(2,1)S(1)}, u32[]{:S(2)}, u32[]{:S(2)}) collective-permute-start(bf16[2,48,6144]{2,1,0:T(8,128)(2,1)S(1)} %get-tuple-element.19), channel_id=1, source_target_pairs={{0,2},{1,3},{2,0},{3,1},{4,6},{5,7},{6,4},{7,5},{8,10},{9,11},{10,... | collective-permute-start | bytes 3538952 | tf_op jit(solution)/shard_map/ppermute | solution.py:21
  40.9 53.0 %collective-permute-start.3 = (bf16[4,48,6144]{2,1,0:T(8,128)(2,1)S(1)}, bf16[4,48,6144]{2,1,0:T(8,128)(2,1)}, u32[]{:S(2)}, u32[]{:S(2)}) collective-permute-start(bf16[4,48,6144]{2,1,0:T(8,128)(2,1)S(1)} %bitcast.174), channel_id=1, source_target_pairs={{0,4},{1,5},{2,6},{3,7},{4,0},{5,1},{6,2},{7,3},{8,12},{9,13},{10,... | collective-permute-start | bytes 7077896 | tf_op jit(solution)/shard_map/ppermute | solution.py:21
  99.3 102.8 %collective-permute-start.4 = (bf16[8,48,6144]{2,1,0:T(8,128)(2,1)}, bf16[8,48,6144]{2,1,0:T(8,128)(2,1)}, u32[]{:S(2)}, u32[]{:S(2)}) collective-permute-start(bf16[8,48,6144]{2,1,0:T(8,128)(2,1)} %bitcast.13), channel_id=1, source_target_pairs={{0,8},{1,9},{2,10},{3,11},{4,12},{5,13},{6,14},{7,15},{8,0},{9,1},... | collective-permute-start | bytes 14155784 | tf_op jit(solution)/shard_map/ppermute | solution.py:21
  210.4 17.0 %copy-start.7 = (f32[2,1536]{1,0:T(2,128)S(1)}, f32[2,1536]{1,0:T(2,128)}, u32[]{:S(2)}) copy-start(f32[2,1536]{1,0:T(2,128)} %param.13) | copy-start | bytes 36868
  210.4 17.0 %copy-start.8 = (f32[2,1536]{1,0:T(2,128)S(1)}, f32[2,1536]{1,0:T(2,128)}, u32[]{:S(2)}) copy-start(f32[2,1536]{1,0:T(2,128)} %param.12) | copy-start | bytes 36868
  210.4 17.1 %copy-start.4 = (bf16[1,384,1536]{2,1,0:T(8,128)(2,1)S(1)}, bf16[1,384,1536]{2,1,0:T(8,128)(2,1)}, u32[]{:S(2)}) copy-start(bf16[1,384,1536]{2,1,0:T(8,128)(2,1)} %param.8) | copy-start | bytes 3538948
  225.3 10.6 %copy-start.9 = (f32[2,768]{1,0:T(2,128)S(1)}, f32[2,768]{1,0:T(2,128)}, u32[]{:S(2)}) copy-start(f32[2,768]{1,0:T(2,128)} %param.15) | copy-start | bytes 18436
  225.3 10.6 %copy-start.10 = (f32[2,768]{1,0:T(2,128)S(1)}, f32[2,768]{1,0:T(2,128)}, u32[]{:S(2)}) copy-start(f32[2,768]{1,0:T(2,128)} %param.14) | copy-start | bytes 18436
  225.3 406.4 %collective-permute-start.5 = (bf16[16,48,6144]{2,1,0:T(8,128)(2,1)}, bf16[16,48,6144]{2,1,0:T(8,128)(2,1)}, u32[]{:S(2)}, u32[]{:S(2)}) collective-permute-start(bf16[16,48,6144]{2,1,0:T(8,128)(2,1)} %bitcast.171), channel_id=1, source_target_pairs={{0,16},{1,17},{2,18},{3,19},{4,20},{5,21},{6,22},{7,23},{8,24},{9,... | collective-permute-start | bytes 28311560 | tf_op jit(solution)/shard_map/ppermute | solution.py:21
  228.5 1.0 copy-start.1
  229.5 442.3 %collective-permute-start.6 = (bf16[8,1536]{1,0:T(8,128)(2,1)S(1)}, bf16[8,1536]{1,0:T(8,128)(2,1)S(1)}, u32[]{:S(2)}, u32[]{:S(2)}) collective-permute-start(bf16[8,1536]{1,0:T(8,128)(2,1)S(1)} %get-tuple-element.17), channel_id=1, source_target_pairs={{4,0},{8,4},{12,8},{16,12},{20,16},{24,20},{28,24},{5,1},{9,5},{13... | collective-permute-start | bytes 73736 | tf_op jit(solution)/shard_map/ppermute | solution.py:42
  230.8 455.1 %collective-permute-start = (bf16[8,1536]{1,0:T(8,128)(2,1)S(1)}, bf16[8,1536]{1,0:T(8,128)(2,1)S(1)}, u32[]{:S(2)}, u32[]{:S(2)}) collective-permute-start(bf16[8,1536]{1,0:T(8,128)(2,1)S(1)} %get-tuple-element.16), channel_id=1, source_target_pairs={{0,4},{4,8},{8,12},{12,16},{16,20},{20,24},{24,28},{1,5},{5,9},{9,... | collective-permute-start | bytes 73736 | tf_op jit(solution)/shard_map/ppermute | solution.py:39
  646.2 10.7 %copy-start = (bf16[2,16,48,6144]{3,2,1,0:T(8,128)(2,1)}, bf16[2,16,48,6144]{3,2,1,0:T(8,128)(2,1)S(1)}, u32[]{:S(2)}) copy-start(bf16[2,16,48,6144]{3,2,1,0:T(8,128)(2,1)S(1)} %reverse_select_fusion) | copy-start | bytes 56623108
  656.9 10.4 %copy-start.5 = (bf16[1,384,1536]{2,1,0:T(8,128)(2,1)S(1)}, bf16[1,384,1536]{2,1,0:T(8,128)(2,1)}, u32[]{:S(2)}) copy-start(bf16[1,384,1536]{2,1,0:T(8,128)(2,1)} %param.8) | copy-start | bytes 3538948
  667.3 4.5 copy-start.2
  685.9 8.6 slice-start
  689.5 5.0 slice-start.1
  693.2 36.6 %copy-start.14 = (f32[384,1536]{1,0:T(8,128)}, f32[384,1536]{1,0:T(8,128)S(1)}, u32[]{:S(2)}) copy-start(f32[384,1536]{1,0:T(8,128)S(1)} %get-tuple-element.25) | copy-start | bytes 7077892
  693.2 7.2 collective-permute-start.8
  695.7 6.3 collective-permute-start.7
  702.0 1.3 copy-start.11
  703.2 3.7 copy-start.15
  711.4 14.0 %collective-permute-start.10 = (bf16[16,768]{1,0:T(8,128)(2,1)S(1)}, bf16[16,768]{1,0:T(8,128)(2,1)S(1)}, u32[]{:S(2)}, u32[]{:S(2)}) collective-permute-start(bf16[16,768]{1,0:T(8,128)(2,1)S(1)} %get-tuple-element.23), channel_id=1, source_target_pairs={{0,4},{4,8},{8,12},{12,16},{16,20},{20,24},{24,28},{1,5},{5,9},{9,... | collective-permute-start | bytes 73736 | tf_op jit(solution)/shard_map/ppermute | solution.py:39
  723.8 6.0 collective-permute-start.9
  732.5 4.1 copy-start.12
  788.3 1.3 copy-start.16
  794.2 9.6 collective-permute-start.12
  802.2 5.9 copy-start.13
  802.2 5.9 collective-permute-start.11
  997.3 1.7 copy-start.3
Sparse Core Ops, SparseCore 0:
  788.5 206.8 reduce-scatter.3
